TPU v7x, 512 devices: a whole 4x8x8 slice. The times are simulated.
512 devices in a mesh: dp: 32 (over x, y), expert: 16 (over z, core).
Axes of the slice: x: 4, y: 8, z: 8, core: 2. Of those that a mesh axis runs over, the one named last changes fastest.
Arguments:
- tokens: bfloat16 [65536, 2048], P(('dp', 'expert')), may hold values from -6 to 6
- cotangent: bfloat16 [65536, 2048], P(('dp', 'expert')), may hold values from -6 to 6
- expert_ids: int32 [65536, 2], P(('dp', 'expert')), may hold values from 0 to 15, as said below
- router_probs: float32 [65536, 2], P(('dp', 'expert')), may hold values from 0.1 to 1
- gate_weight: bfloat16 [16, 2048, 768], P('expert', 'dp'), may hold values from -0.125 to 0.125
- up_weight: bfloat16 [16, 2048, 768], P('expert', 'dp'), may hold values from -0.125 to 0.125
- down_weight: bfloat16 [16, 768, 2048], P('expert', 'dp'), may hold values from -0.21875 to 0.21875
Outputs:
- mixed_out: bfloat16 [65536, 2048], P(('dp', 'expert'))
- grad_tokens: bfloat16 [65536, 2048], P(('dp', 'expert'))
- grad_probs: float32 [65536, 2], P(('dp', 'expert'))
- grad_down: bfloat16 [16, 768, 2048], P('expert', 'dp')
Inputs may be any that keep to these rules, and one draw needn't show every extreme that they name: `expert_ids`: each token names 2 different experts. In each aligned block of 128 tokens (the tokens of one device) no expert is named more than 18 times, and in each aligned group of 16 such blocks one expert is named exactly 18 times in every block of the group.
All inputs are finite; a program needn't handle non-finite values.
Results may differ from a plain program's by a relative error of at most 0.023.
Values may be sent and summed in bfloat16 or wider, within the bound.
No kernel may reach another device: no remote copies, remote signals or barrier semaphores. Data moves between devices by JAX's collectives and lax.ppermute only.
A program may use at most 64 MiB of HBM per device.

v0:
```python
import jax
import jax.numpy as jnp
from jax import lax
from jax.sharding import PartitionSpec as P


def shards(tokens, cotangent, expert_ids, router_probs, gate_weight, up_weight, down_weight):
    tok_count = tokens.shape[0]
    features = tokens.shape[1]
    choices_each = expert_ids.shape[1]
    slot_total = tok_count * choices_each
    groups = lax.axis_size("expert")
    capacity = 9 * slot_total // (8 * groups)
    slot_count = groups * capacity
    flat_ids = expert_ids.reshape(slot_total)
    member = (flat_ids[:, None] == jnp.arange(groups, dtype=jnp.int32)[None, :]).astype(jnp.int32)
    before = jnp.cumsum(member, axis=0) - member
    target = flat_ids * capacity + jnp.sum(before * member, axis=1)
    placer = (target[None, :] == jnp.arange(slot_count, dtype=jnp.int32)[:, None]).astype(
        jnp.bfloat16
    )
    placer_tok = jnp.sum(placer.reshape(slot_count, tok_count, choices_each), axis=2)
    weighted = (
        (router_probs[:, :, None] * cotangent.astype(jnp.float32)[:, None, :])
        .astype(jnp.bfloat16)
        .reshape(slot_total, features)
    )
    send_rows = jnp.dot(placer_tok, tokens, preferred_element_type=jnp.float32).astype(jnp.bfloat16)
    send_grad = jnp.dot(placer, weighted, preferred_element_type=jnp.float32).astype(jnp.bfloat16)
    recv_rows, recv_grad = (
        lax.all_to_all(
            send_rows.reshape(groups, capacity, features),
            "expert",
            split_axis=0,
            concat_axis=0,
            tiled=True,
        ),
        lax.all_to_all(
            send_grad.reshape(groups, capacity, features),
            "expert",
            split_axis=0,
            concat_axis=0,
            tiled=True,
        ),
    )
    x_rows = recv_rows.reshape(slot_count, features)
    dy_rows = recv_grad.reshape(slot_count, features)
    w_gate, w_up = (
        lax.all_gather(gate_weight[0], "dp", axis=0, tiled=True),
        lax.all_gather(up_weight[0], "dp", axis=0, tiled=True),
    )
    gate_pre = jnp.dot(x_rows, w_gate, preferred_element_type=jnp.float32)
    up_pre = jnp.dot(x_rows, w_up, preferred_element_type=jnp.float32)
    sig_gate = jax.nn.sigmoid(gate_pre)
    active = gate_pre * sig_gate
    hidden = (active * up_pre).astype(jnp.bfloat16)
    contract = (((1,), (1,)), ((), ()))
    weight_rows = lax.all_gather(down_weight[0], "dp", axis=0, tiled=True)
    part_hidden = hidden
    acc_part = jnp.dot(part_hidden, weight_rows, preferred_element_type=jnp.float32)
    back_part = lax.dot_general(dy_rows, weight_rows, contract, preferred_element_type=jnp.float32)
    output = acc_part.astype(jnp.bfloat16)
    grad_gate = (back_part * up_pre * sig_gate * (1.0 + gate_pre * (1.0 - sig_gate))).astype(
        jnp.bfloat16
    )
    grad_up = (back_part * active).astype(jnp.bfloat16)
    grad_rows = (
        lax.dot_general(grad_gate, w_gate, contract, preferred_element_type=jnp.float32)
        + lax.dot_general(grad_up, w_up, contract, preferred_element_type=jnp.float32)
    ).astype(jnp.bfloat16)
    back_out, back_grad = (
        lax.all_to_all(
            output.reshape(groups, capacity, features),
            "expert",
            split_axis=0,
            concat_axis=0,
            tiled=True,
        ),
        lax.all_to_all(
            grad_rows.reshape(groups, capacity, features),
            "expert",
            split_axis=0,
            concat_axis=0,
            tiled=True,
        ),
    )
    unplace = (((0,), (0,)), ((), ()))
    gathered = lax.dot_general(
        placer, back_out.reshape(slot_count, features), unplace, preferred_element_type=jnp.float32
    )
    gathered = gathered.reshape(tok_count, choices_each, features)
    grad_tokens = lax.dot_general(
        placer_tok,
        back_grad.reshape(slot_count, features),
        unplace,
        preferred_element_type=jnp.float32,
    ).astype(jnp.bfloat16)
    mixed_out = jnp.sum(router_probs[:, :, None] * gathered, axis=1).astype(jnp.bfloat16)
    grad_probs = jnp.sum(cotangent.astype(jnp.float32)[:, None, :] * gathered, axis=2)
    part_hidden = hidden
    grad_down = lax.psum_scatter(
        lax.dot_general(
            part_hidden, dy_rows, (((0,), (0,)), ((), ())), preferred_element_type=jnp.float32
        ).astype(jnp.bfloat16),
        "dp",
        scatter_dimension=0,
        tiled=True,
    )[None]
    return (mixed_out, grad_tokens, grad_probs, grad_down)


def solution(mesh):
    placed = (
        P(("dp", "expert"), None),
        P(("dp", "expert"), None),
        P(("dp", "expert"), None),
        P(("dp", "expert"), None),
        P("expert", "dp", None),
        P("expert", "dp", None),
        P("expert", "dp", None),
    )
    return jax.shard_map(
        shards,
        mesh=mesh,
        in_specs=placed,
        out_specs=(
            P(("dp", "expert"), None),
            P(("dp", "expert"), None),
            P(("dp", "expert"), None),
            P("expert", "dp", None),
        ),
        check_vma=False,
    )
```

profile of v0, /device:TPU:16, one launch (start us, length us, event | category | flops | bytes accessed | tf_op | source)
XLA Modules:
  0.0 505.6 jit_solution(4395308883108628984)
XLA Ops:
  14.2 10.6 %all-to-all-start = ((bf16[16,18,2048]{2,1,0:T(8,128)(2,1)}), bf16[16,18,2048]{2,1,0:T(8,128)(2,1)}, u32[]{:S(2)}, u32[]{:S(2)}) async-start(bf16[16,18,2048]{2,1,0:T(8,128)(2,1)} %reshape.96), calls=%async_computation | async-start | bytes 3145728 | tf_op jit(solution)/shard_map/all_to_all | solution.py:31
  26.1 2.5 mul.84
  28.6 2.1 convolution_convert_fusion.2
  30.7 1.4 reshape.100
  32.1 30.6 %all-to-all-done = bf16[16,18,2048]{2,1,0:T(8,128)(2,1)} async-done(((bf16[16,18,2048]{2,1,0:T(8,128)(2,1)}), bf16[16,18,2048]{2,1,0:T(8,128)(2,1)}, u32[]{:S(2)}, u32[]{:S(2)}) %all-to-all-start) | async-done | bytes 1179680 | tf_op jit(solution)/shard_map/all_to_all | solution.py:31
  62.7 4.8 all-to-all-start.2
  67.5 2.4 reshape.97
  70.0 35.4 %all-to-all-done.2 = bf16[16,18,2048]{2,1,0:T(8,128)(2,1)S(1)} async-done(((bf16[16,18,2048]{2,1,0:T(8,128)(2,1)}), bf16[16,18,2048]{2,1,0:T(8,128)(2,1)S(1)}, u32[]{:S(2)}, u32[]{:S(2)}) %all-to-all-start.2) | async-done | bytes 1179680 | tf_op jit(solution)/shard_map/all_to_all | solution.py:38
  106.6 4.3 fusion.10
  110.9 73.5 %all-gather.9.cloned.1.call-done = bf16[1,2048,768]{2,1,0:T(8,128)(2,1)} async-done(((bf16[1,64,768]{2,1,0:T(8,128)(2,1)}), bf16[1,2048,768]{2,1,0:T(8,128)(2,1)}) %all-gather.9.cloned.1.call-update) | async-done | bytes 3145744 | tf_op jit(solution)/shard_map/all_gather | solution.py:50
  184.4 4.1 multiply_convert_fusion.4
  189.3 3.6 convolution_convert_fusion
  192.9 76.5 %all-gather.11.cloned.1.call-done = bf16[1,768,2048]{2,1,0:T(8,128)(2,1)} async-done(((bf16[1,24,2048]{2,1,0:T(8,128)(2,1)}), bf16[1,768,2048]{2,1,0:T(8,128)(2,1)}) %all-gather.11.cloned.1.call-update) | async-done | bytes 3145744 | tf_op jit(solution)/shard_map/all_gather | solution.py:58
  269.4 3.0 fusion.18
  273.7 7.5 %all-to-all-start.1 = ((bf16[16,18,2048]{2,1,0:T(8,128)(2,1)}), bf16[16,18,2048]{2,1,0:T(8,128)(2,1)S(1)}, u32[]{:S(2)}, u32[]{:S(2)}) async-start(bf16[16,18,2048]{2,1,0:T(8,128)(2,1)} %reshape.98), calls=%async_computation.1 | async-start | bytes 3145728 | tf_op jit(solution)/shard_map/all_to_all | solution.py:72
  281.2 3.5 fusion
  286.9 2.2 fusion.15
  289.1 2.4 reshape.102
  291.5 27.6 %all-to-all-done.1 = bf16[16,18,2048]{2,1,0:T(8,128)(2,1)S(1)} async-done(((bf16[16,18,2048]{2,1,0:T(8,128)(2,1)}), bf16[16,18,2048]{2,1,0:T(8,128)(2,1)S(1)}, u32[]{:S(2)}, u32[]{:S(2)}) %all-to-all-start.1) | async-done | bytes 1179680 | tf_op jit(solution)/shard_map/all_to_all | solution.py:72
  319.1 4.8 all-to-all-start.3
  326.2 35.6 %all-to-all-done.3 = bf16[16,18,2048]{2,1,0:T(8,128)(2,1)} async-done(((bf16[16,18,2048]{2,1,0:T(8,128)(2,1)}), bf16[16,18,2048]{2,1,0:T(8,128)(2,1)}, u32[]{:S(2)}, u32[]{:S(2)}) %all-to-all-start.3) | async-done | bytes 1179680 | tf_op jit(solution)/shard_map/all_to_all | solution.py:79
  361.8 1.6 reshape.103
  363.4 3.0 multiply_reduce_fusion
  367.7 131.4 %reduce-scatter.2.cloned.1.call-done = bf16[24,2048]{1,0:T(8,128)(2,1)} async-done(((bf16[768,2048]{1,0:T(8,128)(2,1)}), bf16[24,2048]{1,0:T(8,128)(2,1)}) %reduce-scatter.2.cloned.1.call-update) | async-done | bytes 98320 | tf_op jit(solution)/shard_map/reduce_scatter | solution.py:101
  (58 shorter events, 17.2 us)
Async XLA Ops:
  7.2 5.2 %copy-start = (bf16[128,2048]{1,0:T(8,128)(2,1)S(1)}, bf16[128,2048]{1,0:T(8,128)(2,1)}, u32[]{:S(2)}) copy-start(bf16[128,2048]{1,0:T(8,128)(2,1)} %param.7) | copy-start | bytes 1572868
  7.2 99.4 %all-gather.7.cloned.1.call-start = ((), (), s32[]{:S(2)}) async-start(), calls=%async_computation.6 | async-start | bytes 3244032 | tf_op jit(solution)/shard_map/all_gather | solution.py:49
  7.9 176.5 %all-gather.9.cloned.1.call-start = ((), (), s32[]{:S(2)}) async-start(), calls=%async_computation.7 | async-start | bytes 3244032 | tf_op jit(solution)/shard_map/all_gather | solution.py:50
  8.7 260.7 %all-gather.11.cloned.1.call-start = ((), (), s32[]{:S(2)}) async-start(), calls=%async_computation.8 | async-start | bytes 3244032 | tf_op jit(solution)/shard_map/all_gather | solution.py:58
  14.2 10.6 %copy-start.5 = (f32[128,2]{0,1:T(2,128)S(1)}, f32[128,2]{0,1:T(2,128)}, u32[]{:S(2)}) copy-start(f32[128,2]{0,1:T(2,128)} %param.10) | copy-start | bytes 3076
  14.2 10.9 %copy-start.1 = (bf16[128,2048]{1,0:T(8,128)(2,1)S(1)}, bf16[128,2048]{1,0:T(8,128)(2,1)}, u32[]{:S(2)}) copy-start(bf16[128,2048]{1,0:T(8,128)(2,1)} %param.8) | copy-start | bytes 1572868
  14.2 48.5 %all-to-all-start = ((bf16[16,18,2048]{2,1,0:T(8,128)(2,1)}), bf16[16,18,2048]{2,1,0:T(8,128)(2,1)}, u32[]{:S(2)}, u32[]{:S(2)}) async-start(bf16[16,18,2048]{2,1,0:T(8,128)(2,1)} %reshape.96), calls=%async_computation | async-start | bytes 3145728 | tf_op jit(solution)/shard_map/all_to_all | solution.py:31
  62.7 42.7 %all-to-all-start.2 = ((bf16[16,18,2048]{2,1,0:T(8,128)(2,1)}), bf16[16,18,2048]{2,1,0:T(8,128)(2,1)S(1)}, u32[]{:S(2)}, u32[]{:S(2)}) async-start(bf16[16,18,2048]{2,1,0:T(8,128)(2,1)} %reshape.100), calls=%async_computation.2 | async-start | bytes 3145728 | tf_op jit(solution)/shard_map/all_to_all | solution.py:38
  67.5 431.6 %reduce-scatter.2.cloned.1.call-start = ((), (), s32[]{:S(2)}) async-start(), calls=%async_computation.5 | async-start | bytes 3244032 | tf_op jit(solution)/shard_map/reduce_scatter | solution.py:101
  106.6 77.8 %copy-start.3 = (bf16[288,2048]{1,0:T(8,128)(2,1)S(1)}, bf16[288,2048]{1,0:T(8,128)(2,1)}, u32[]{:S(2)}) copy-start(bf16[288,2048]{1,0:T(8,128)(2,1)} %reshape.97) | copy-start | bytes 3538948
  110.9 78.4 %copy-start.2 = (bf16[288,2048]{1,0:T(8,128)(2,1)S(1)}, bf16[288,2048]{1,0:T(8,128)(2,1)}, u32[]{:S(2)}) copy-start(bf16[288,2048]{1,0:T(8,128)(2,1)} %reshape.101) | copy-start | bytes 3538948
  188.5 0.8 copy-start.10
  192.9 76.5 %copy-start.11 = (bf16[288,768]{1,0:T(8,128)(2,1)S(1)}, bf16[288,768]{1,0:T(8,128)(2,1)}, u32[]{:S(2)}) copy-start(bf16[288,768]{1,0:T(8,128)(2,1)} %copy-done.10) | copy-start | bytes 1327108
  273.7 45.3 %all-to-all-start.1 = ((bf16[16,18,2048]{2,1,0:T(8,128)(2,1)}), bf16[16,18,2048]{2,1,0:T(8,128)(2,1)S(1)}, u32[]{:S(2)}, u32[]{:S(2)}) async-start(bf16[16,18,2048]{2,1,0:T(8,128)(2,1)} %reshape.98), calls=%async_computation.1 | async-start | bytes 3145728 | tf_op jit(solution)/shard_map/all_to_all | solution.py:72
  281.2 3.5 copy-start.7
  281.2 3.5 copy-start.8
  284.8 1.9 copy-start.6
  284.8 2.1 copy-start.9
  319.1 42.8 %all-to-all-start.3 = ((bf16[16,18,2048]{2,1,0:T(8,128)(2,1)}), bf16[16,18,2048]{2,1,0:T(8,128)(2,1)}, u32[]{:S(2)}, u32[]{:S(2)}) async-start(bf16[16,18,2048]{2,1,0:T(8,128)(2,1)} %reshape.102), calls=%async_computation.3 | async-start | bytes 3145728 | tf_op jit(solution)/shard_map/all_to_all | solution.py:79
  326.2 37.2 %copy-start.4 = (bf16[288,2048,1]{1,0,2:T(8,128)(2,1)S(1)}, bf16[288,2048,1]{1,0,2:T(8,128)(2,1)}, u32[]{:S(2)}) copy-start(bf16[288,2048,1]{1,0,2:T(8,128)(2,1)} %reshape.107) | copy-start | bytes 3538948
Sparse Core Ops, SparseCore 0:
  11.1 88.1 all-gather.6
  102.5 81.7 all-gather.8
  187.6 81.7 all-gather.10
  274.3 224.7 reduce-scatter.1
where the time goes:
time: 506 us
  waiting for transfers between devices  413 us (82%)
  matrix products  28.8 us (6%)
  starting transfers between devices  27.9 us (6%)
  local copies, waits for them, and re-layouts  19.8 us (4%)
  between operations  14 us (3%)
    reduce_scatter x1, waiting for transfers between devices, shards(): lax.psum_scatter(lax.dot_general(part_hidden, dy_rows, (((0,), (0,)), (()...  131 us
    all_gather x1, waiting for transfers between devices, shards(): weight_rows = lax.all_gather(down_weight[0], 'dp', axis=0, tiled=True)  76.5 us
    all_gather x1, waiting for transfers between devices, shards(): lax.all_gather(up_weight[0], 'dp', axis=0, tiled=True)  73.5 us
    all_to_all x1, waiting for transfers between devices, shards(): lax.all_to_all(grad_rows.reshape(groups, capacity, features), 'expert', s...  35.6 us
    all_to_all x1, waiting for transfers between devices, shards(): lax.all_to_all(send_grad.reshape(groups, capacity, features), 'expert', s...  35.4 us
    all_to_all x1, waiting for transfers between devices, shards(): lax.all_to_all(send_rows.reshape(groups, capacity, features), 'expert', s...  30.6 us
    all_to_all x1, waiting for transfers between devices, shards(): lax.all_to_all(output.reshape(groups, capacity, features), 'expert', spli...  27.6 us
    all_to_all x1, starting transfers between devices, shards(): lax.all_to_all(send_rows.reshape(groups, capacity, features), 'expert', s...  10.6 us
  transfers between devices with their start and end apart: 8, of which 7 were waited for; matrix products, arithmetic and copies ran while one was open for 10% of the time, Pallas kernels for 0%

commit v1 on v0

--- a/solution.py
+++ b/solution.py
@@ -55,7 +55,11 @@
     active = gate_pre * sig_gate
     hidden = (active * up_pre).astype(jnp.bfloat16)
     contract = (((1,), (1,)), ((), ()))
-    weight_rows = lax.all_gather(down_weight[0], "dp", axis=0, tiled=True)
+    chunk = down_weight[0]
+    views = []
+    for _ in range(lax.axis_size("dp")):
+        views.append(chunk)
+    weight_rows = jnp.concatenate(lax.all_to_all(jnp.stack(views), "dp", 0, 0), 0)
     part_hidden = hidden
     acc_part = jnp.dot(part_hidden, weight_rows, preferred_element_type=jnp.float32)
     back_part = lax.dot_general(dy_rows, weight_rows, contract, preferred_element_type=jnp.float32)

time: 506 us -> 449 us (0.89)
  waiting for transfers between devices: 413 us -> 346 us
  starting transfers between devices: 27.9 us -> 35.5 us
    all_gather x1 -> x0, waiting for transfers between devices: 76.5 us -> none  [shards(): weight_rows = lax.all_gather(down_weight[0], 'dp', axis=0, tiled=True)]
    all_gather x1, waiting for transfers between devices: 73.5 us -> 85.6 us  [shards(): lax.all_gather(up_weight[0], 'dp', axis=0, tiled=True)]
    all_to_all x0 -> x1, starting transfers between devices: none -> 10.1 us  [shards(): lax.all_to_all(jnp.stack(views), 'dp', 0, 0)]
  transfers between devices with their start and end apart: 8 -> 8, of which waited for: 7 -> 6; matrix products, arithmetic and copies ran while one was open for 10% -> 11% of each run, Pallas kernels for 0% -> 0%
where the time goes in v1:
time: 449 us; the launch traced here: 448 us
  waiting for transfers between devices  346 us (77%)
  starting transfers between devices  35.5 us (8%)
  matrix products  27.9 us (6%)
  local copies, waits for them, and re-layouts  22 us (5%)
  between operations  14 us (3%)
    reduce_scatter x1, waiting for transfers between devices, shards(): lax.psum_scatter(lax.dot_general(part_hidden, dy_rows, (((0,), (0,)), (()...  127 us
    all_gather x1, waiting for transfers between devices, shards(): lax.all_gather(up_weight[0], 'dp', axis=0, tiled=True)  85.6 us
    all_to_all x1, waiting for transfers between devices, shards(): lax.all_to_all(send_grad.reshape(groups, capacity, features), 'expert', s...  37.1 us
    all_to_all x1, waiting for transfers between devices, shards(): lax.all_to_all(grad_rows.reshape(groups, capacity, features), 'expert', s...  36.4 us
    all_to_all x1, waiting for transfers between devices, shards(): lax.all_to_all(send_rows.reshape(groups, capacity, features), 'expert', s...  30.6 us
    all_to_all x1, waiting for transfers between devices, shards(): lax.all_to_all(output.reshape(groups, capacity, features), 'expert', spli...  27.5 us
    all_to_all x1, starting transfers between devices, shards(): lax.all_to_all(send_rows.reshape(groups, capacity, features), 'expert', s...  10.6 us
    all_to_all x1, starting transfers between devices, shards(): lax.all_to_all(jnp.stack(views), 'dp', 0, 0)  10.1 us
  transfers between devices with their start and end apart: 8, of which 6 were waited for; matrix products, arithmetic and copies ran while one was open for 11% of the time, Pallas kernels for 0%

profile of v1, /device:TPU:16, one launch (start us, length us, event | category | flops | bytes accessed | tf_op | source)
XLA Modules:
  0.0 448.0 jit_solution(17510027363975098561)
XLA Ops:
  12.7 10.6 %all-to-all-start = ((bf16[16,18,2048]{2,1,0:T(8,128)(2,1)}), bf16[16,18,2048]{2,1,0:T(8,128)(2,1)}, u32[]{:S(2)}, u32[]{:S(2)}) async-start(bf16[16,18,2048]{2,1,0:T(8,128)(2,1)} %reshape.100), calls=%async_computation | async-start | bytes 3145728 | tf_op jit(solution)/shard_map/all_to_all | solution.py:31
  24.4 2.4 mul.84
  27.1 2.1 convolution_convert_fusion.2
  30.6 30.6 %all-to-all-done = bf16[16,18,2048]{2,1,0:T(8,128)(2,1)} async-done(((bf16[16,18,2048]{2,1,0:T(8,128)(2,1)}), bf16[16,18,2048]{2,1,0:T(8,128)(2,1)}, u32[]{:S(2)}, u32[]{:S(2)}) %all-to-all-start) | async-done | bytes 1179680 | tf_op jit(solution)/shard_map/all_to_all | solution.py:31
  61.3 4.8 %all-to-all-start.3 = ((bf16[16,18,2048]{2,1,0:T(8,128)(2,1)}), bf16[16,18,2048]{2,1,0:T(8,128)(2,1)S(1)}, u32[]{:S(2)}, u32[]{:S(2)}) async-start(bf16[16,18,2048]{2,1,0:T(8,128)(2,1)} %reshape.105), calls=%async_computation.3 | async-start | bytes 3145728 | tf_op jit(solution)/shard_map/all_to_all | solution.py:38
  66.8 37.1 %all-to-all-done.3 = bf16[16,18,2048]{2,1,0:T(8,128)(2,1)S(1)} async-done(((bf16[16,18,2048]{2,1,0:T(8,128)(2,1)}), bf16[16,18,2048]{2,1,0:T(8,128)(2,1)S(1)}, u32[]{:S(2)}, u32[]{:S(2)}) %all-to-all-start.3) | async-done | bytes 1179680 | tf_op jit(solution)/shard_map/all_to_all | solution.py:38
  103.9 2.0 stack.3
  105.9 10.1 %all-to-all-start.1 = ((bf16[32,24,2048]{2,1,0:T(8,128)(2,1)}), bf16[32,24,2048]{2,1,0:T(8,128)(2,1)}, u32[]{:S(2)}, u32[]{:S(2)}) async-start(bf16[32,24,2048]{2,1,0:T(8,128)(2,1)} %stack.3), calls=%async_computation.1 | async-start | bytes 6291456 | tf_op jit(solution)/shard_map/all_to_all | solution.py:62
  116.1 2.4 reshape.101
  119.7 3.3 fusion.6
  123.1 85.6 %all-gather.7.cloned.1.call-done = bf16[1,2048,768]{2,1,0:T(8,128)(2,1)} async-done(((bf16[1,64,768]{2,1,0:T(8,128)(2,1)}), bf16[1,2048,768]{2,1,0:T(8,128)(2,1)}) %all-gather.7.cloned.1.call-update) | async-done | bytes 3145744 | tf_op jit(solution)/shard_map/all_gather | solution.py:50
  208.7 4.2 multiply_convert_fusion.4
  213.7 3.5 convolution_convert_fusion
  218.3 3.0 convolution_convert_fusion.3
  222.6 5.1 %all-to-all-start.2 = ((bf16[16,18,2048]{2,1,0:T(8,128)(2,1)}), bf16[16,18,2048]{2,1,0:T(8,128)(2,1)S(1)}, u32[]{:S(2)}, u32[]{:S(2)}) async-start(bf16[16,18,2048]{2,1,0:T(8,128)(2,1)} %reshape.103), calls=%async_computation.2 | async-start | bytes 3145728 | tf_op jit(solution)/shard_map/all_to_all | solution.py:76
  227.7 3.6 fusion.31
  233.4 2.2 fusion.11
  235.7 2.4 reshape.107
  238.1 27.5 %all-to-all-done.2 = bf16[16,18,2048]{2,1,0:T(8,128)(2,1)S(1)} async-done(((bf16[16,18,2048]{2,1,0:T(8,128)(2,1)}), bf16[16,18,2048]{2,1,0:T(8,128)(2,1)S(1)}, u32[]{:S(2)}, u32[]{:S(2)}) %all-to-all-start.2) | async-done | bytes 1179680 | tf_op jit(solution)/shard_map/all_to_all | solution.py:76
  265.6 4.8 %all-to-all-start.4 = ((bf16[16,18,2048]{2,1,0:T(8,128)(2,1)}), bf16[16,18,2048]{2,1,0:T(8,128)(2,1)}, u32[]{:S(2)}, u32[]{:S(2)}) async-start(bf16[16,18,2048]{2,1,0:T(8,128)(2,1)} %reshape.107), calls=%async_computation.4 | async-start | bytes 3145728 | tf_op jit(solution)/shard_map/all_to_all | solution.py:83
  271.9 36.4 %all-to-all-done.4 = bf16[16,18,2048]{2,1,0:T(8,128)(2,1)} async-done(((bf16[16,18,2048]{2,1,0:T(8,128)(2,1)}), bf16[16,18,2048]{2,1,0:T(8,128)(2,1)}, u32[]{:S(2)}, u32[]{:S(2)}) %all-to-all-start.4) | async-done | bytes 1179680 | tf_op jit(solution)/shard_map/all_to_all | solution.py:83
  308.3 1.6 reshape.108
  309.9 3.0 multiply_reduce_fusion
  314.2 127.3 %reduce-scatter.2.cloned.1.call-done = bf16[24,2048]{1,0:T(8,128)(2,1)} async-done(((bf16[768,2048]{1,0:T(8,128)(2,1)}), bf16[24,2048]{1,0:T(8,128)(2,1)}) %reduce-scatter.2.cloned.1.call-update) | async-done | bytes 98320 | tf_op jit(solution)/shard_map/reduce_scatter | solution.py:105
  (58 shorter events, 18.1 us)
Async XLA Ops:
  7.2 3.7 copy-start
  7.2 112.6 %all-gather.5.cloned.1.call-start = ((), (), s32[]{:S(2)}) async-start(), calls=%async_computation.7 | async-start | bytes 3244032 | tf_op jit(solution)/shard_map/all_gather | solution.py:49
  12.7 10.6 %copy-start.1 = (bf16[128,2048]{1,0:T(8,128)(2,1)S(1)}, bf16[128,2048]{1,0:T(8,128)(2,1)}, u32[]{:S(2)}) copy-start(bf16[128,2048]{1,0:T(8,128)(2,1)} %param.8) | copy-start | bytes 1572868
  12.7 48.5 %all-to-all-start = ((bf16[16,18,2048]{2,1,0:T(8,128)(2,1)}), bf16[16,18,2048]{2,1,0:T(8,128)(2,1)}, u32[]{:S(2)}, u32[]{:S(2)}) async-start(bf16[16,18,2048]{2,1,0:T(8,128)(2,1)} %reshape.100), calls=%async_computation | async-start | bytes 3145728 | tf_op jit(solution)/shard_map/all_to_all | solution.py:31
  24.4 2.4 copy-start.4
  30.6 73.3 %copy-start.3 = (bf16[1,24,2048]{2,1,0:T(8,128)(2,1)S(1)}, bf16[1,24,2048]{2,1,0:T(8,128)(2,1)}, u32[]{:S(2)}) copy-start(bf16[1,24,2048]{2,1,0:T(8,128)(2,1)} %param.13) | copy-start | bytes 294916
  61.3 42.7 %all-to-all-start.3 = ((bf16[16,18,2048]{2,1,0:T(8,128)(2,1)}), bf16[16,18,2048]{2,1,0:T(8,128)(2,1)S(1)}, u32[]{:S(2)}, u32[]{:S(2)}) async-start(bf16[16,18,2048]{2,1,0:T(8,128)(2,1)} %reshape.105), calls=%async_computation.3 | async-start | bytes 3145728 | tf_op jit(solution)/shard_map/all_to_all | solution.py:38
  66.1 142.6 %all-gather.7.cloned.1.call-start = ((), (), s32[]{:S(2)}) async-start(), calls=%async_computation.8 | async-start | bytes 3244032 | tf_op jit(solution)/shard_map/all_gather | solution.py:50
  105.9 111.3 %all-to-all-start.1 = ((bf16[32,24,2048]{2,1,0:T(8,128)(2,1)}), bf16[32,24,2048]{2,1,0:T(8,128)(2,1)}, u32[]{:S(2)}, u32[]{:S(2)}) async-start(bf16[32,24,2048]{2,1,0:T(8,128)(2,1)} %stack.3), calls=%async_computation.1 | async-start | bytes 6291456 | tf_op jit(solution)/shard_map/all_to_all | solution.py:62
  116.1 325.4 %reduce-scatter.2.cloned.1.call-start = ((), (), s32[]{:S(2)}) async-start(), calls=%async_computation.6 | async-start | bytes 3244032 | tf_op jit(solution)/shard_map/reduce_scatter | solution.py:105
  123.1 89.9 %copy-start.7 = (f32[288,768]{1,0:T(8,128)}, f32[288,768]{1,0:T(8,128)S(1)}, u32[]{:S(2)}) copy-start(f32[288,768]{1,0:T(8,128)S(1)} %fusion.6) | copy-start | bytes 2654212
  123.1 90.6 %copy-start.2 = (bf16[288,2048]{1,0:T(8,128)(2,1)S(1)}, bf16[288,2048]{1,0:T(8,128)(2,1)}, u32[]{:S(2)}) copy-start(bf16[288,2048]{1,0:T(8,128)(2,1)} %reshape.106) | copy-start | bytes 3538948
  213.0 0.8 copy-start.10
  217.3 1.0 copy-start.11
  222.6 42.9 %all-to-all-start.2 = ((bf16[16,18,2048]{2,1,0:T(8,128)(2,1)}), bf16[16,18,2048]{2,1,0:T(8,128)(2,1)S(1)}, u32[]{:S(2)}, u32[]{:S(2)}) async-start(bf16[16,18,2048]{2,1,0:T(8,128)(2,1)} %reshape.103), calls=%async_computation.2 | async-start | bytes 3145728 | tf_op jit(solution)/shard_map/all_to_all | solution.py:76
  227.7 3.6 copy-start.6
  227.7 3.6 copy-start.8
  231.3 1.9 copy-start.5
  231.3 2.1 copy-start.9
  265.6 42.8 %all-to-all-start.4 = ((bf16[16,18,2048]{2,1,0:T(8,128)(2,1)}), bf16[16,18,2048]{2,1,0:T(8,128)(2,1)}, u32[]{:S(2)}, u32[]{:S(2)}) async-start(bf16[16,18,2048]{2,1,0:T(8,128)(2,1)} %reshape.107), calls=%async_computation.4 | async-start | bytes 3145728 | tf_op jit(solution)/shard_map/all_to_all | solution.py:83
Sparse Core Ops, SparseCore 0:
  11.1 88.1 all-gather.4
  102.5 106.1 all-gather.6
  217.4 224.0 reduce-scatter.1
